TPU v7x, 512 devices: a whole 4x8x8 slice. The times are simulated.
512 devices in a mesh: tensor: 8 (over y), expert: 64 (over x, z, core).
Axes of the slice: x: 4, y: 8, z: 8, core: 2. Of those that a mesh axis runs over, the one named last changes fastest.
Arguments:
- attn_partial: bfloat16 [8, 4096, 4096], P('tensor', 'expert'), may hold values from -6 to 6
- norm_gain: float32 [4096], replicated, may hold values from 0.1 to 1.9
- expert_ids: int32 [4096, 8], P('expert'), may hold values from 0 to 63, all different within a row; in each aligned block of 8 rows (0 to 7, 8 to 15, ...) at most 2 rows name the same one
- route_weights: float32 [4096, 8], P('expert'), may hold values from 0.1 to 1
- gate_proj: bfloat16 [64, 4096, 1024], P('expert', None, 'tensor'), may hold values from -0.09375 to 0.09375
- up_proj: bfloat16 [64, 4096, 1024], P('expert', None, 'tensor'), may hold values from -0.09375 to 0.09375
- down_proj: bfloat16 [64, 1024, 4096], P('expert', None, 'tensor'), may hold values from -0.1875 to 0.1875
Outputs:
- combined: bfloat16 [4096, 4096], P(('expert', 'tensor'))
Inputs may be any that keep to these rules, and one draw needn't show every extreme that they name: `expert_ids`: each row names 8 different experts. In each aligned block of 8 rows (the rows of one device in the output's order) no expert is named by more than 2 rows, a bound that some block reaches.
All inputs are finite; a program needn't handle non-finite values.
Results may differ from a plain program's by a relative error of at most 0.025.
Values may be sent and summed in bfloat16 or wider, within the bound.
No kernel may reach another device: no remote copies, remote signals or barrier semaphores. Data moves between devices by JAX's collectives and lax.ppermute only.
A program may use at most 64 MiB of HBM per device.

v0:
```python
import jax
import jax.numpy as jnp
from jax import lax
from jax.sharding import PartitionSpec as P

QB = 128


def normalize_dequant(summed, norm_gain, block_width):
    row_count, feature_width = summed.shape
    mean_sq = jnp.mean(summed * summed, axis=-1, keepdims=True)
    normed = summed * lax.rsqrt(mean_sq + 1e-06) * norm_gain
    blocks = normed.reshape(row_count, feature_width // block_width, block_width)
    scales = ((jnp.max(jnp.abs(blocks), axis=-1) + 1e-06) / 448.0).astype(jnp.bfloat16)
    scale_f = scales.astype(jnp.float32)[:, :, None]
    values = (blocks / scale_f).astype(jnp.bfloat16)
    restored = (values.astype(jnp.float32) * scale_f).astype(jnp.bfloat16)
    return restored.reshape(row_count, feature_width)


def on_device(attn_partial, norm_gain, expert_ids, route_weights, gate_proj, up_proj, down_proj):
    tensor_count = lax.axis_size("tensor")
    expert_count = lax.axis_size("expert")
    tensor_index = lax.axis_index("tensor")
    group_tokens = expert_ids.shape[0]
    top_count = expert_ids.shape[1]
    row_count = group_tokens // tensor_count
    feature_width = attn_partial.shape[2]
    capacity = max(2, (2 * row_count * top_count + expert_count - 1) // expert_count)
    gate_matrix = gate_proj[0]
    up_matrix = up_proj[0]
    down_matrix = down_proj[0]
    column_share = down_matrix.shape[1]
    own_start = tensor_index * row_count
    own_ids = lax.dynamic_slice_in_dim(expert_ids, own_start, row_count, 0)
    own_weights = lax.dynamic_slice_in_dim(route_weights, own_start, row_count, 0)
    parts = lax.all_to_all(
        attn_partial[0].reshape(tensor_count, row_count, feature_width),
        "tensor",
        split_axis=0,
        concat_axis=0,
        tiled=True,
    )
    summed = jnp.sum(parts.astype(jnp.float32), axis=0)
    restored = normalize_dequant(summed, norm_gain, QB)
    labels = jnp.arange(expert_count, dtype=jnp.int32)
    hit = own_ids[..., None] == labels
    member = jnp.sum(hit.astype(jnp.int32), axis=1)
    earlier = jnp.cumsum(member, axis=0) - member
    places = jnp.arange(capacity, dtype=jnp.int32)
    chosen = (earlier[..., None] == places) & (member[..., None] > 0)
    send = jnp.einsum(
        "rec,rd->ecd", chosen.astype(jnp.bfloat16), restored, preferred_element_type=jnp.float32
    ).astype(jnp.bfloat16)
    recv = lax.all_to_all(send, "expert", split_axis=0, concat_axis=0, tiled=True)
    rows = lax.all_gather(recv, "tensor", axis=0, tiled=False)
    slot_total = tensor_count * expert_count * capacity
    rows = rows.reshape(slot_total, feature_width)
    gate_act = jnp.dot(rows, gate_matrix, preferred_element_type=jnp.float32)
    up_act = jnp.dot(rows, up_matrix, preferred_element_type=jnp.float32)
    hidden = (jax.nn.silu(gate_act) * up_act).astype(jnp.bfloat16)
    expert_sum = jnp.dot(
        lax.all_gather(hidden, "tensor", axis=1, tiled=True),
        down_matrix,
        preferred_element_type=jnp.float32,
    )
    expert_rows = expert_sum.astype(jnp.bfloat16).reshape(
        tensor_count, expert_count, capacity, column_share
    )
    returned = lax.all_to_all(
        lax.all_to_all(expert_rows, "tensor", split_axis=0, concat_axis=3, tiled=True),
        "expert",
        split_axis=1,
        concat_axis=1,
        tiled=True,
    )
    returned = returned.reshape(expert_count, capacity, feature_width)
    pair_weight = jnp.sum(jnp.where(hit, own_weights[..., None], 0.0), axis=1)
    mixing = jnp.where(chosen, pair_weight[..., None], 0.0)
    combined = jnp.einsum(
        "rec,ecd->rd", mixing, returned.astype(jnp.float32), precision=lax.Precision.HIGHEST
    )
    return combined.astype(jnp.bfloat16)


def solution(mesh):
    return jax.shard_map(
        on_device,
        mesh=mesh,
        in_specs=(
            P("tensor", "expert", None),
            P(),
            P("expert", None),
            P("expert", None),
            P("expert", None, "tensor"),
            P("expert", None, "tensor"),
            P("expert", None, "tensor"),
        ),
        out_specs=P(("expert", "tensor"), None),
        check_vma=False,
    )
```

profile of v0, /device:TPU:1, one launch (start us, length us, event | category | flops | bytes accessed | tf_op | source)
XLA Modules:
  0.0 320.2 jit_solution(14053400340128236630)
XLA Ops:
  6.5 0.0 copy-start
  6.5 7.8 %all-to-all-start = ((bf16[8,8,4096]{2,1,0:T(8,128)(2,1)}), bf16[8,8,4096]{2,1,0:T(8,128)(2,1)S(1)}, u32[]{:S(2)}, u32[]{:S(2)}) async-start(bf16[8,8,4096]{2,1,0:T(8,128)(2,1)} %bitcast.51), calls=%async_computation | async-start | bytes 1048576 | tf_op jit(solution)/shard_map/all_to_all | solution.py:37
  14.3 0.0 all-gather.6.cloned.1.call-start
  14.4 0.8 constant_dynamic-slice_fusion.1
  15.1 0.1 copy.36
  15.2 0.1 convert_reduce_fusion.1
  15.3 13.9 %all-to-all-done = bf16[8,8,4096]{2,1,0:T(8,128)(2,1)S(1)} async-done(((bf16[8,8,4096]{2,1,0:T(8,128)(2,1)}), bf16[8,8,4096]{2,1,0:T(8,128)(2,1)S(1)}, u32[]{:S(2)}, u32[]{:S(2)}) %all-to-all-start) | async-done | bytes 524320 | tf_op jit(solution)/shard_map/all_to_all | solution.py:37
  29.3 0.1 convert_reduce_fusion
  29.3 0.1 multiply_reduce_fusion
  29.5 0.9 fusion.12
  30.4 0.1 copy.38
  30.5 0.1 copy.39
  30.6 1.2 convolution_convert_fusion
  31.8 1.1 copy.40
  32.9 45.3 %all_to_all.33 = bf16[64,2,4096]{2,1,0:T(2,128)(2,1)} all-to-all(bf16[64,2,4096]{2,1,0:T(2,128)(2,1)S(1)} %copy.40), channel_id=1, replica_groups=mesh['tensor'=8,'expert'=64] {'expert'}, dimensions={0} | all-to-all | bytes 2097152 | tf_op jit(solution)/shard_map/all_to_all | solution.py:55
  78.1 0.0 all-gather.6.cloned.1.call-update
  78.2 0.0 copy-start.3
  78.2 0.0 all-gather.4.cloned.1.call-start
  78.2 87.9 %all-gather.6.cloned.1.call-done = bf16[512,2,4096]{2,1,0:T(2,128)(2,1)} async-done(((bf16[64,2,4096]{2,1,0:T(2,128)(2,1)}), bf16[512,2,4096]{2,1,0:T(2,128)(2,1)}) %all-gather.6.cloned.1.call-update) | async-done | bytes 8388624 | tf_op jit(solution)/shard_map/all_gather | solution.py:56
  166.1 13.1 %reshape.59 = bf16[1024,4096]{1,0:T(8,128)(2,1)} reshape(bf16[512,2,4096]{2,1,0:T(2,128)(2,1)} %all-gather.6.cloned.1.call-done) | data formatting | bytes 16777216 | tf_op jit(solution)/shard_map/reshape | solution.py:58
  179.2 0.0 copy-done.3
  179.2 0.0 copy-start.1
  179.2 0.0 copy-start.4
  179.2 5.9 %fusion.5 = f32[1024,128]{1,0:T(8,128)S(1)} fusion(bf16[1024,4096]{1,0:T(8,128)(2,1)} %reshape.59, bf16[1,4096,128]{2,1,0:T(8,128)(2,1)S(1)} %copy-done.3), kind=kOutput, calls=%fused_computation.9 | convolution fusion | flops 1073741824 | bytes 9961472 | tf_op jit(solution)/shard_map/dot_general | solution.py:59
  185.1 0.0 copy-done.1
  185.1 0.1 copy-done.4
  185.2 3.1 fusion.1
  188.3 0.0 all-gather.4.cloned.1.call-update
  188.3 0.0 copy-start.2
  188.3 44.5 %all-gather.4.cloned.1.call-done = bf16[1024,1024]{1,0:T(8,128)(2,1)} async-done(((bf16[1024,128]{1,0:T(8,128)(2,1)}), bf16[1024,1024]{1,0:T(8,128)(2,1)}) %all-gather.4.cloned.1.call-update) | async-done | bytes 2097168 | tf_op jit(solution)/shard_map/all_gather | solution.py:63
  232.8 0.0 copy-done
  232.8 2.8 convolution_convert_fusion.1
  235.7 0.4 reshape.60
  236.1 25.8 %all_to_all.34 = bf16[8,64,2,512]{3,2,1,0:T(2,128)(2,1)S(1)} all-to-all(bf16[8,64,2,512]{3,2,1,0:T(2,128)(2,1)S(1)} %reshape.60), channel_id=1, replica_groups=mesh['tensor'=8,'expert'=64] {'tensor'}, dimensions={0} | all-to-all | bytes 2097152 | tf_op jit(solution)/shard_map/all_to_all | solution.py:71
  261.9 1.1 copy.41
  263.0 1.6 all_to_all.27
  264.6 18.1 %all-to-all-start.3 = ((bf16[1,64,2,4096]{3,2,0,1:T(2,128)(2,1)}), bf16[1,64,2,4096]{3,2,0,1:T(2,128)(2,1)S(1)}, u32[]{:S(2)}, u32[]{:S(2)}) async-start(bf16[1,64,2,4096]{3,2,0,1:T(2,128)(2,1)} %all_to_all.27), calls=%async_computation.3 | async-start | bytes 2097152 | tf_op jit(solution)/shard_map/all_to_all | solution.py:70
  282.7 0.0 copy-done.2
  282.7 0.1 constant_dynamic-slice_fusion
  282.8 0.1 copy.37
  282.9 0.1 select_reduce_fusion
  282.9 28.3 %all-to-all-done.3 = bf16[1,64,2,4096]{3,2,0,1:T(2,128)(2,1)S(1)} async-done(((bf16[1,64,2,4096]{3,2,0,1:T(2,128)(2,1)}), bf16[1,64,2,4096]{3,2,0,1:T(2,128)(2,1)S(1)}, u32[]{:S(2)}, u32[]{:S(2)}) %all-to-all-start.3) | async-done | bytes 1048608 | tf_op jit(solution)/shard_map/all_to_all | solution.py:70
  311.2 2.2 fusion
  (5 shorter events, 0.1 us)
Async XLA Ops:
  6.5 226.3 %copy-start = (bf16[1,1024,512]{2,1,0:T(8,128)(2,1)S(1)}, bf16[1,1024,512]{2,1,0:T(8,128)(2,1)}, u32[]{:S(2)}) copy-start(bf16[1,1024,512]{2,1,0:T(8,128)(2,1)} %param.13) | copy-start | bytes 3145732
  6.5 22.7 %all-to-all-start = ((bf16[8,8,4096]{2,1,0:T(8,128)(2,1)}), bf16[8,8,4096]{2,1,0:T(8,128)(2,1)S(1)}, u32[]{:S(2)}, u32[]{:S(2)}) async-start(bf16[8,8,4096]{2,1,0:T(8,128)(2,1)} %bitcast.51), calls=%async_computation | async-start | bytes 1048576 | tf_op jit(solution)/shard_map/all_to_all | solution.py:37
  14.3 151.8 %all-gather.6.cloned.1.call-start = ((), (), s32[]{:S(2)}) async-start(), calls=%async_computation.5 | async-start | bytes 9437184 | tf_op jit(solution)/shard_map/all_gather | solution.py:56
  78.2 101.1 %copy-start.3 = (bf16[1,4096,128]{2,1,0:T(8,128)(2,1)S(1)}, bf16[1,4096,128]{2,1,0:T(8,128)(2,1)}, u32[]{:S(2)}) copy-start(bf16[1,4096,128]{2,1,0:T(8,128)(2,1)} %param.11) | copy-start | bytes 3145732
  78.2 154.6 %all-gather.4.cloned.1.call-start = ((), (), s32[]{:S(2)}) async-start(), calls=%async_computation.4 | async-start | bytes 2359296 | tf_op jit(solution)/shard_map/all_gather | solution.py:63
  179.2 5.9 %copy-start.1 = (bf16[1024,4096]{1,0:T(8,128)(2,1)S(1)}, bf16[1024,4096]{1,0:T(8,128)(2,1)}, u32[]{:S(2)}) copy-start(bf16[1024,4096]{1,0:T(8,128)(2,1)} %reshape.59) | copy-start | bytes 25165828
  179.2 6.0 %copy-start.4 = (bf16[1,4096,128]{2,1,0:T(8,128)(2,1)S(1)}, bf16[1,4096,128]{2,1,0:T(8,128)(2,1)}, u32[]{:S(2)}) copy-start(bf16[1,4096,128]{2,1,0:T(8,128)(2,1)} %param.12) | copy-start | bytes 3145732
  188.3 94.4 %copy-start.2 = (f32[64,8]{0,1:T(8,128)S(1)}, f32[64,8]{0,1:T(8,128)}, u32[]{:S(2)}) copy-start(f32[64,8]{0,1:T(8,128)} %param.10) | copy-start | bytes 6148
  264.6 46.6 %all-to-all-start.3 = ((bf16[1,64,2,4096]{3,2,0,1:T(2,128)(2,1)}), bf16[1,64,2,4096]{3,2,0,1:T(2,128)(2,1)S(1)}, u32[]{:S(2)}, u32[]{:S(2)}) async-start(bf16[1,64,2,4096]{3,2,0,1:T(2,128)(2,1)} %all_to_all.27), calls=%async_computation.3 | async-start | bytes 2097152 | tf_op jit(solution)/shard_map/all_to_all | solution.py:70
Sparse Core Ops, SparseCore 0:
  78.3 87.8 all-gather.5
  188.4 44.3 all-gather.3
where the time goes:
time: 321 us; the launch traced here: 320 us
  waiting for transfers between devices  175 us (55%)
  blocking collectives  71 us (22%)
  starting transfers between devices  25.9 us (8%)
  local copies, waits for them, and re-layouts  18.6 us (6%)
  matrix products  15.1 us (5%)
  between operations  13.5 us (4%)
    all_gather x1, waiting for transfers between devices, on_device(): rows = lax.all_gather(recv, 'tensor', axis=0, tiled=False)  87.9 us
    all_to_all x1, blocking collectives, on_device(): lax.all_to_all(send, 'expert', split_axis=0, concat_axis=0, tiled=True)  45.3 us
    all_gather x1, waiting for transfers between devices, on_device(): lax.all_gather(hidden, 'tensor', axis=1, tiled=True)  44.5 us
    all_to_all x1, waiting for transfers between devices, on_device(): lax.all_to_all(lax.all_to_all(expert_rows, 'tensor', split_axis=0, concat...  28.3 us
    all_to_all x1, blocking collectives, on_device(): lax.all_to_all(expert_rows, 'tensor', split_axis=0, concat_axis=3, tiled=...  25.8 us
    all_to_all x1, starting transfers between devices, on_device(): lax.all_to_all(lax.all_to_all(expert_rows, 'tensor', split_axis=0, concat...  18.1 us
    all_to_all x1, waiting for transfers between devices, on_device(): lax.all_to_all(attn_partial[0].reshape(tensor_count, row_count, feature_w...  13.9 us
    reshape x1, local copies, waits for them, and re-layouts, on_device(): rows = rows.reshape(slot_total, feature_width)  13.1 us
  transfers between devices with their start and end apart: 4, of which 4 were waited for; matrix products, arithmetic and copies ran while one was open for 0% of the time, Pallas kernels for 0%

commit v1 on v0

--- a/solution.py
+++ b/solution.py
@@ -1,9 +1,34 @@
+import functools
 import jax
 import jax.numpy as jnp
 from jax import lax
 from jax.sharding import PartitionSpec as P
 
 QB = 128
+
+
+def list_blocks(shard_in, mesh_dim):
+    local_part = lax.axis_index(mesh_dim)
+    f_next = lax.axis_size(mesh_dim)
+    met_up, front, r2 = (f_next, local_part, shard_in.shape[1])
+    later = tuple((rr * met_up if it == 1 else rr for it, rr in enumerate(shard_in.shape)))
+    oldest = jnp.zeros(later, shard_in.dtype)
+    back = lax.dynamic_update_slice_in_dim(oldest, shard_in, front * r2, axis=1)
+    known = row_out = shard_in
+    for ix in range(1, met_up // 2 + 1):
+        k_now = tuple(((it, (it + 1) % met_up) for it in range(met_up)))
+        known = lax.ppermute(known, axis_name=mesh_dim, perm=k_now)
+        back = lax.dynamic_update_slice_in_dim(back, known, (front - ix) % met_up * r2, axis=1)
+        if 2 * ix < met_up:
+            block_now = tuple(((it, (it - 1) % met_up) for it in range(met_up)))
+            row_out = lax.ppermute(row_out, axis_name=mesh_dim, perm=block_now)
+            back = lax.dynamic_update_slice_in_dim(
+                back, row_out, (front + ix) % met_up * r2, axis=1
+            )
+    return back
+
+
+positions_prepare = functools.partial(list_blocks, mesh_dim="tensor")
 
 
 def normalize_dequant(summed, norm_gain, block_width):
@@ -59,11 +84,7 @@
     gate_act = jnp.dot(rows, gate_matrix, preferred_element_type=jnp.float32)
     up_act = jnp.dot(rows, up_matrix, preferred_element_type=jnp.float32)
     hidden = (jax.nn.silu(gate_act) * up_act).astype(jnp.bfloat16)
-    expert_sum = jnp.dot(
-        lax.all_gather(hidden, "tensor", axis=1, tiled=True),
-        down_matrix,
-        preferred_element_type=jnp.float32,
-    )
+    expert_sum = jnp.dot(positions_prepare(hidden), down_matrix, preferred_element_type=jnp.float32)
     expert_rows = expert_sum.astype(jnp.bfloat16).reshape(
         tensor_count, expert_count, capacity, column_share
     )

time: 321 us -> 314 us (0.978)
  waiting for transfers between devices: 175 us -> 143 us
  starting transfers between devices: 25.9 us -> 45.7 us
  local copies, waits for them, and re-layouts: 18.6 us -> 23.2 us
    all_gather x1 -> x0, waiting for transfers between devices: 44.5 us -> none  [on_device(): lax.all_gather(hidden, 'tensor', axis=1, tiled=True)]
    ppermute x0 -> x7, starting transfers between devices: none -> 21.4 us  [the longest x3 13.7 us: list_blocks(): row_out = lax.ppermute(row_out, axis_name=mesh_dim, perm=block_now)]
    ppermute x0 -> x7, waiting for transfers between devices: none -> 12.8 us  [the longest x4 12.7 us: list_blocks(): known = lax.ppermute(known, axis_name=mesh_dim, perm=k_now)]
    dynamic_update_slice x0 -> x7, local copies, waits for them, and re-layouts: none -> 3.46 us  [the longest x4 2.25 us: list_blocks(): lax.dynamic_update_slice_in_dim(back, known, (front - ix) % met_up * r2,...]
  transfers between devices with their start and end apart: 4 -> 10, of which waited for: 4 -> 7; matrix products, arithmetic and copies ran while one was open for 0% -> 1% of each run, Pallas kernels for 0% -> 0%
where the time goes in v1:
time: 314 us; the launch traced here: 313 us
  waiting for transfers between devices  143 us (46%)
  blocking collectives  72.8 us (23%)
  starting transfers between devices  45.7 us (15%)
  local copies, waits for them, and re-layouts  23.2 us (7%)
  between operations  13.8 us (4%)
  matrix products  13.2 us (4%)
    all_gather x1, waiting for transfers between devices, on_device(): rows = lax.all_gather(recv, 'tensor', axis=0, tiled=False)  88 us
    all_to_all x1, blocking collectives, on_device(): lax.all_to_all(send, 'expert', split_axis=0, concat_axis=0, tiled=True)  45.3 us
    all_to_all x1, waiting for transfers between devices, on_device(): lax.all_to_all(lax.all_to_all(expert_rows, 'tensor', split_axis=0, concat...  28.3 us
    all_to_all x1, blocking collectives, on_device(): lax.all_to_all(expert_rows, 'tensor', split_axis=0, concat_axis=3, tiled=...  27.5 us
    all_to_all x1, starting transfers between devices, on_device(): lax.all_to_all(lax.all_to_all(expert_rows, 'tensor', split_axis=0, concat...  16.5 us
    all_to_all x1, waiting for transfers between devices, on_device(): lax.all_to_all(attn_partial[0].reshape(tensor_count, row_count, feature_w...  13.9 us
    ppermute x3, starting transfers between devices, list_blocks(): row_out = lax.ppermute(row_out, axis_name=mesh_dim, perm=block_now)  13.7 us
    reshape x1, local copies, waits for them, and re-layouts, on_device(): rows = rows.reshape(slot_total, feature_width)  13.1 us
  transfers between devices with their start and end apart: 10, of which 7 were waited for; matrix products, arithmetic and copies ran while one was open for 1% of the time, Pallas kernels for 0%

profile of v1, /device:TPU:1, one launch (start us, length us, event | category | flops | bytes accessed | tf_op | source)
XLA Modules:
  0.0 313.0 jit_solution(572868152509308433)
XLA Ops:
  6.5 0.0 copy-start
  6.5 0.0 copy-start.2
  6.5 7.8 %all-to-all-start = ((bf16[8,8,4096]{2,1,0:T(8,128)(2,1)}), bf16[8,8,4096]{2,1,0:T(8,128)(2,1)S(1)}, u32[]{:S(2)}, u32[]{:S(2)}) async-start(bf16[8,8,4096]{2,1,0:T(8,128)(2,1)} %bitcast.53), calls=%async_computation | async-start | bytes 1048576 | tf_op jit(solution)/shard_map/all_to_all | solution.py:62
  14.3 0.0 all-gather.3.cloned.1.call-start
  14.4 0.8 constant_dynamic-slice_fusion.1
  15.1 0.1 copy.36
  15.2 0.1 convert_reduce_fusion.1
  15.3 13.9 %all-to-all-done = bf16[8,8,4096]{2,1,0:T(8,128)(2,1)S(1)} async-done(((bf16[8,8,4096]{2,1,0:T(8,128)(2,1)}), bf16[8,8,4096]{2,1,0:T(8,128)(2,1)S(1)}, u32[]{:S(2)}, u32[]{:S(2)}) %all-to-all-start) | async-done | bytes 524320 | tf_op jit(solution)/shard_map/all_to_all | solution.py:62
  29.3 0.1 convert_reduce_fusion
  29.3 0.1 multiply_reduce_fusion
  29.5 0.9 fusion.12
  30.4 0.1 copy.38
  30.5 0.1 copy.39
  30.6 0.0 copy-done.2
  30.6 0.5 convolution_convert_fusion
  31.1 1.1 copy.40
  32.2 45.3 %all_to_all.33 = bf16[64,2,4096]{2,1,0:T(2,128)(2,1)} all-to-all(bf16[64,2,4096]{2,1,0:T(2,128)(2,1)S(1)} %copy.40), channel_id=1, replica_groups=mesh['tensor'=8,'expert'=64] {'expert'}, dimensions={0} | all-to-all | bytes 2097152 | tf_op jit(solution)/shard_map/all_to_all | solution.py:80
  77.4 0.0 all-gather.3.cloned.1.call-update
  77.5 0.0 copy-start.4
  77.5 88.0 %all-gather.3.cloned.1.call-done = bf16[512,2,4096]{2,1,0:T(2,128)(2,1)} async-done(((bf16[64,2,4096]{2,1,0:T(2,128)(2,1)}), bf16[512,2,4096]{2,1,0:T(2,128)(2,1)}) %all-gather.3.cloned.1.call-update) | async-done | bytes 8388624 | tf_op jit(solution)/shard_map/all_gather | solution.py:81
  165.4 13.1 %reshape.59 = bf16[1024,4096]{1,0:T(8,128)(2,1)} reshape(bf16[512,2,4096]{2,1,0:T(2,128)(2,1)} %all-gather.3.cloned.1.call-done) | data formatting | bytes 16777216 | tf_op jit(solution)/shard_map/reshape | solution.py:83
  178.5 0.0 copy-done.4
  178.5 0.0 copy-start.1
  178.5 5.9 %fusion.5 = f32[1024,128]{1,0:T(8,128)S(1)} fusion(bf16[1024,4096]{1,0:T(8,128)(2,1)} %reshape.59, bf16[1,4096,128]{2,1,0:T(8,128)(2,1)S(1)} %copy-done.4), kind=kOutput, calls=%fused_computation.9 | convolution fusion | flops 1073741824 | bytes 9961472 | tf_op jit(solution)/shard_map/dot_general | solution.py:84
  184.4 0.3 broadcast_in_dim.41
  184.7 0.0 copy-done
  184.7 0.0 copy-done.1
  184.7 2.4 constant_dynamic-update-slice_fusion.7
  187.1 1.9 collective-permute-start
  189.0 4.6 %collective-permute-start.1 = (bf16[1024,128]{1,0:T(8,128)(2,1)S(1)}, bf16[1024,128]{1,0:T(8,128)(2,1)}, u32[]{:S(2)}, u32[]{:S(2)}) collective-permute-start(bf16[1024,128]{1,0:T(8,128)(2,1)S(1)} %get-tuple-element.6), channel_id=1, source_target_pairs={{0,448},{64,0},{128,64},{192,128},{256,192},{320,256},{384,320},{4... | collective-permute-start | bytes 786440 | tf_op jit(solution)/shard_map/ppermute | solution.py:24
  193.6 3.7 %collective-permute-done = bf16[1024,128]{1,0:T(8,128)(2,1)} collective-permute-done((bf16[1024,128]{1,0:T(8,128)(2,1)S(1)}, bf16[1024,128]{1,0:T(8,128)(2,1)}, u32[]{:S(2)}, u32[]{:S(2)}) %collective-permute-start) | collective-permute-done | bytes 262176 | tf_op jit(solution)/shard_map/ppermute | solution.py:20
  197.4 1.9 collective-permute-start.2
  199.3 0.0 collective-permute-done.1
  199.3 4.6 %collective-permute-start.3 = (bf16[1024,128]{1,0:T(8,128)(2,1)}, bf16[1024,128]{1,0:T(8,128)(2,1)S(1)}, u32[]{:S(2)}, u32[]{:S(2)}) collective-permute-start(bf16[1024,128]{1,0:T(8,128)(2,1)} %collective-permute-done.1), channel_id=1, source_target_pairs={{0,448},{64,0},{128,64},{192,128},{256,192},{320,256},{384,320},{4... | collective-permute-start | bytes 786440 | tf_op jit(solution)/shard_map/ppermute | solution.py:24
  204.0 0.0 copy-start.5
  204.0 2.9 collective-permute-done.2
  206.9 1.9 collective-permute-start.4
  208.9 1.0 constant_dynamic-update-slice_fusion.6
  209.9 1.0 constant_dynamic-update-slice_fusion.5
  210.9 0.0 collective-permute-done.3
  211.0 4.6 %collective-permute-start.5 = (bf16[1024,128]{1,0:T(8,128)(2,1)S(1)}, bf16[1024,128]{1,0:T(8,128)(2,1)S(1)}, u32[]{:S(2)}, u32[]{:S(2)}) collective-permute-start(bf16[1024,128]{1,0:T(8,128)(2,1)S(1)} %collective-permute-done.3), channel_id=1, source_target_pairs={{0,448},{64,0},{128,64},{192,128},{256,192},{320,256},{384,320},{4... | collective-permute-start | bytes 786440 | tf_op jit(solution)/shard_map/ppermute | solution.py:24
  215.5 1.0 constant_dynamic-update-slice_fusion.4
  216.6 0.0 collective-permute-done.4
  216.6 1.9 collective-permute-start.6
  218.5 0.1 constant_dynamic-update-slice_fusion.3
  218.6 0.1 constant_dynamic-update-slice_fusion.2
  218.7 0.1 collective-permute-done.5
  218.8 0.1 constant_dynamic-update-slice_fusion.1
  218.9 6.0 %collective-permute-done.6 = bf16[1024,128]{1,0:T(8,128)(2,1)S(1)} collective-permute-done((bf16[1024,128]{1,0:T(8,128)(2,1)S(1)}, bf16[1024,128]{1,0:T(8,128)(2,1)S(1)}, u32[]{:S(2)}, u32[]{:S(2)}) %collective-permute-start.6) | collective-permute-done | bytes 262176 | tf_op jit(solution)/shard_map/ppermute | solution.py:20
  224.9 0.1 constant_dynamic-update-slice_fusion
  225.0 0.0 copy-done.5
  225.0 2.2 convolution_convert_fusion.1
  227.2 1.5 reshape.60
  228.7 27.5 %all_to_all.34 = bf16[8,64,2,512]{3,2,1,0:T(2,128)(2,1)S(1)} all-to-all(bf16[8,64,2,512]{3,2,1,0:T(2,128)(2,1)S(1)} %reshape.60), channel_id=1, replica_groups=mesh['tensor'=8,'expert'=64] {'tensor'}, dimensions={0} | all-to-all | bytes 2097152 | tf_op jit(solution)/shard_map/all_to_all | solution.py:92
  256.2 1.1 copy.41
  257.4 0.0 copy-start.3
  257.4 1.6 all_to_all.27
  258.9 16.5 %all-to-all-start.3 = ((bf16[1,64,2,4096]{3,2,0,1:T(2,128)(2,1)}), bf16[1,64,2,4096]{3,2,0,1:T(2,128)(2,1)S(1)}, u32[]{:S(2)}, u32[]{:S(2)}) async-start(bf16[1,64,2,4096]{3,2,0,1:T(2,128)(2,1)} %all_to_all.27), calls=%async_computation.3 | async-start | bytes 2097152 | tf_op jit(solution)/shard_map/all_to_all | solution.py:91
  275.4 0.0 copy-done.3
  275.4 0.1 constant_dynamic-slice_fusion
  275.5 0.1 copy.37
  275.6 0.1 select_reduce_fusion
  275.7 28.3 %all-to-all-done.3 = bf16[1,64,2,4096]{3,2,0,1:T(2,128)(2,1)S(1)} async-done(((bf16[1,64,2,4096]{3,2,0,1:T(2,128)(2,1)}), bf16[1,64,2,4096]{3,2,0,1:T(2,128)(2,1)S(1)}, u32[]{:S(2)}, u32[]{:S(2)}) %all-to-all-start.3) | async-done | bytes 1048608 | tf_op jit(solution)/shard_map/all_to_all | solution.py:91
  304.0 2.2 fusion
  (5 shorter events, 0.1 us)
Async XLA Ops:
  6.5 178.1 %copy-start = (bf16[1,4096,128]{2,1,0:T(8,128)(2,1)S(1)}, bf16[1,4096,128]{2,1,0:T(8,128)(2,1)}, u32[]{:S(2)}) copy-start(bf16[1,4096,128]{2,1,0:T(8,128)(2,1)} %param.12) | copy-start | bytes 3145732
  6.5 24.0 %copy-start.2 = (f32[4096]{0:T(1024)S(1)}, f32[4096]{0:T(1024)}, u32[]{:S(2)}) copy-start(f32[4096]{0:T(1024)} %param.8) | copy-start | bytes 49156
  6.5 22.7 %all-to-all-start = ((bf16[8,8,4096]{2,1,0:T(8,128)(2,1)}), bf16[8,8,4096]{2,1,0:T(8,128)(2,1)S(1)}, u32[]{:S(2)}, u32[]{:S(2)}) async-start(bf16[8,8,4096]{2,1,0:T(8,128)(2,1)} %bitcast.53), calls=%async_computation | async-start | bytes 1048576 | tf_op jit(solution)/shard_map/all_to_all | solution.py:62
  14.3 151.1 %all-gather.3.cloned.1.call-start = ((), (), s32[]{:S(2)}) async-start(), calls=%async_computation.4 | async-start | bytes 9437184 | tf_op jit(solution)/shard_map/all_gather | solution.py:81
  77.5 101.1 %copy-start.4 = (bf16[1,4096,128]{2,1,0:T(8,128)(2,1)S(1)}, bf16[1,4096,128]{2,1,0:T(8,128)(2,1)}, u32[]{:S(2)}) copy-start(bf16[1,4096,128]{2,1,0:T(8,128)(2,1)} %param.11) | copy-start | bytes 3145732
  178.5 6.1 %copy-start.1 = (bf16[1024,4096]{1,0:T(8,128)(2,1)S(1)}, bf16[1024,4096]{1,0:T(8,128)(2,1)}, u32[]{:S(2)}) copy-start(bf16[1024,4096]{1,0:T(8,128)(2,1)} %reshape.59) | copy-start | bytes 25165828
  187.1 10.2 %collective-permute-start = (bf16[1024,128]{1,0:T(8,128)(2,1)S(1)}, bf16[1024,128]{1,0:T(8,128)(2,1)}, u32[]{:S(2)}, u32[]{:S(2)}) collective-permute-start(bf16[1024,128]{1,0:T(8,128)(2,1)S(1)} %get-tuple-element.6), channel_id=1, source_target_pairs={{0,64},{64,128},{128,192},{192,256},{256,320},{320,384},{384,448},... | collective-permute-start | bytes 786440 | tf_op jit(solution)/shard_map/ppermute | solution.py:20
  189.0 10.2 %collective-permute-start.1 = (bf16[1024,128]{1,0:T(8,128)(2,1)S(1)}, bf16[1024,128]{1,0:T(8,128)(2,1)}, u32[]{:S(2)}, u32[]{:S(2)}) collective-permute-start(bf16[1024,128]{1,0:T(8,128)(2,1)S(1)} %get-tuple-element.6), channel_id=1, source_target_pairs={{0,448},{64,0},{128,64},{192,128},{256,192},{320,256},{384,320},{4... | collective-permute-start | bytes 786440 | tf_op jit(solution)/shard_map/ppermute | solution.py:24
  197.4 9.6 %collective-permute-start.2 = (bf16[1024,128]{1,0:T(8,128)(2,1)}, bf16[1024,128]{1,0:T(8,128)(2,1)}, u32[]{:S(2)}, u32[]{:S(2)}) collective-permute-start(bf16[1024,128]{1,0:T(8,128)(2,1)} %collective-permute-done), channel_id=1, source_target_pairs={{0,64},{64,128},{128,192},{192,256},{256,320},{320,384},{384,448},... | collective-permute-start | bytes 786440 | tf_op jit(solution)/shard_map/ppermute | solution.py:20
  199.3 11.7 %collective-permute-start.3 = (bf16[1024,128]{1,0:T(8,128)(2,1)}, bf16[1024,128]{1,0:T(8,128)(2,1)S(1)}, u32[]{:S(2)}, u32[]{:S(2)}) collective-permute-start(bf16[1024,128]{1,0:T(8,128)(2,1)} %collective-permute-done.1), channel_id=1, source_target_pairs={{0,448},{64,0},{128,64},{192,128},{256,192},{320,256},{384,320},{4... | collective-permute-start | bytes 786440 | tf_op jit(solution)/shard_map/ppermute | solution.py:24
  204.0 21.0 %copy-start.5 = (bf16[1,1024,512]{2,1,0:T(8,128)(2,1)S(1)}, bf16[1,1024,512]{2,1,0:T(8,128)(2,1)}, u32[]{:S(2)}) copy-start(bf16[1,1024,512]{2,1,0:T(8,128)(2,1)} %param.13) | copy-start | bytes 3145732
  206.9 9.6 %collective-permute-start.4 = (bf16[1024,128]{1,0:T(8,128)(2,1)}, bf16[1024,128]{1,0:T(8,128)(2,1)S(1)}, u32[]{:S(2)}, u32[]{:S(2)}) collective-permute-start(bf16[1024,128]{1,0:T(8,128)(2,1)} %collective-permute-done.2), channel_id=1, source_target_pairs={{0,64},{64,128},{128,192},{192,256},{256,320},{320,384},{384,448},... | collective-permute-start | bytes 786440 | tf_op jit(solution)/shard_map/ppermute | solution.py:20
  211.0 7.9 %collective-permute-start.5 = (bf16[1024,128]{1,0:T(8,128)(2,1)S(1)}, bf16[1024,128]{1,0:T(8,128)(2,1)S(1)}, u32[]{:S(2)}, u32[]{:S(2)}) collective-permute-start(bf16[1024,128]{1,0:T(8,128)(2,1)S(1)} %collective-permute-done.3), channel_id=1, source_target_pairs={{0,448},{64,0},{128,64},{192,128},{256,192},{320,256},{384,320},{4... | collective-permute-start | bytes 786440 | tf_op jit(solution)/shard_map/ppermute | solution.py:24
  216.6 8.3 %collective-permute-start.6 = (bf16[1024,128]{1,0:T(8,128)(2,1)S(1)}, bf16[1024,128]{1,0:T(8,128)(2,1)S(1)}, u32[]{:S(2)}, u32[]{:S(2)}) collective-permute-start(bf16[1024,128]{1,0:T(8,128)(2,1)S(1)} %collective-permute-done.4), channel_id=1, source_target_pairs={{0,64},{64,128},{128,192},{192,256},{256,320},{320,384},{384,448},... | collective-permute-start | bytes 786440 | tf_op jit(solution)/shard_map/ppermute | solution.py:20
  257.4 18.1 %copy-start.3 = (f32[64,8]{0,1:T(8,128)S(1)}, f32[64,8]{0,1:T(8,128)}, u32[]{:S(2)}) copy-start(f32[64,8]{0,1:T(8,128)} %param.10) | copy-start | bytes 6148
  258.9 45.0 %all-to-all-start.3 = ((bf16[1,64,2,4096]{3,2,0,1:T(2,128)(2,1)}), bf16[1,64,2,4096]{3,2,0,1:T(2,128)(2,1)S(1)}, u32[]{:S(2)}, u32[]{:S(2)}) async-start(bf16[1,64,2,4096]{3,2,0,1:T(2,128)(2,1)} %all_to_all.27), calls=%async_computation.3 | async-start | bytes 2097152 | tf_op jit(solution)/shard_map/all_to_all | solution.py:91
Sparse Core Ops, SparseCore 0:
  77.6 87.8 all-gather.2
